TPU v7x, 512 devices: a whole 4x4x16 slice. The times are simulated.
512 devices in a mesh: dp: 8 (over x, core), tensor: 64 (over z, y).
Axes of the slice: x: 4, y: 4, z: 16, core: 2. Of those that a mesh axis runs over, the one named last changes fastest.
Arguments:
- states: bfloat16 [65536, 2048], P(('dp', 'tensor')), may hold values from -150 to 150
- norm_gain: float32 [2048], replicated, may hold values from 0.1 to 1.9
- norm_bias: float32 [2048], replicated, may hold values from -3 to 3
- head_table: bfloat16 [250880, 2048], P('tensor', 'dp'), may hold values from -2 to 2
- seq_lengths: int32 [8], P('dp'), may hold values from 4096 to 8192
- scored_index: int32 [2048], P('dp'), may hold values from 0 to 8191
- targets: int32 [2048], P('dp'), may hold values from 0 to 250879
- slot_mask: int32 [2048], P('dp'), may hold values 0 or 1
Outputs:
- logprob: float32 [2048], P(('dp', 'tensor'))
- entropy: float32 [2048], P(('dp', 'tensor'))
All inputs are finite; a program needn't handle non-finite values. No bound on the sum of `slot_mask` on one device may be relied on, other than what follows from the above.
Results may differ from a plain program's by a relative error of at most 0.012.
The roundings to bfloat16 on the way count: a program that leaves them out, or rounds other values in their place, can miss the bound.
Values may be sent and summed in bfloat16 or wider, within the bound.
No kernel may reach another device: no remote copies, remote signals or barrier semaphores. Data moves between devices by JAX's collectives and lax.ppermute only.
A program may use at most 64 MiB of HBM per device.

v0:
```python
import jax
import jax.numpy as jnp
from jax import lax
from jax.sharding import Mesh, PartitionSpec as P

EPSILON = 1e-05
TENSOR = ("tz", "ty")


def layer_norm(states, norm_gain, norm_bias):
    values = states.astype(jnp.float32)
    center = jnp.mean(values, axis=1, keepdims=True)
    shifted = values - center
    variance = jnp.mean(shifted * shifted, axis=1, keepdims=True)
    return (shifted * lax.rsqrt(variance + EPSILON) * norm_gain + norm_bias).astype(jnp.bfloat16)


def contract_last(left, right):
    return lax.dot_general(
        left, right, (((1,), (1,)), ((), ())), preferred_element_type=jnp.float32
    )


def body(states, norm_gain, norm_bias, head_table, seq_lengths, scored_index, targets, slot_mask):
    local_rows = states.shape[0]
    devices = lax.axis_size(TENSOR)
    position = lax.axis_index(TENSOR)
    first_row = position * local_rows
    scored_count = scored_index.shape[0]
    owned_count = scored_count // devices
    offset = position * owned_count
    width = states.shape[1]
    row_iota = jnp.arange(local_rows, dtype=jnp.int32)
    picker = (scored_index[:, None] - first_row == row_iota[None, :]).astype(jnp.bfloat16)
    picked = jnp.dot(picker, states, preferred_element_type=jnp.float32).astype(jnp.bfloat16)
    ring = lax.axis_size("ty")
    by_y = picked.reshape(devices // ring, ring, owned_count, width).transpose(1, 0, 2, 3)
    near = lax.all_to_all(by_y, "ty", 0, 0, tiled=True)
    near = jnp.sum(near.astype(jnp.float32), axis=0).astype(jnp.bfloat16)
    arrived = lax.all_to_all(near, "tz", 0, 0, tiled=True)
    owned_rows = jnp.sum(arrived.astype(jnp.float32), axis=0)
    owned_normed = layer_norm(owned_rows, norm_gain, norm_bias)
    along_z = lax.all_to_all(
        jnp.broadcast_to(owned_normed[None], (devices // ring, owned_count, width)),
        "tz",
        0,
        0,
        tiled=True,
    )
    along_y = lax.all_to_all(
        jnp.broadcast_to(along_z[None], (ring, devices // ring, owned_count, width)),
        "ty",
        0,
        0,
        tiled=True,
    )
    chosen = along_y.transpose(1, 0, 2, 3).reshape(scored_count, width)
    vocab_local = head_table.shape[0]
    split = vocab_local // 32 * 16
    local_target = targets - position * vocab_local
    parts = []
    for low, high in ((0, split), (split, vocab_local)):
        logits = contract_last(
            chosen, lax.all_gather(head_table[low:high], "dp", axis=1, tiled=True)
        )
        vocab_iota = jnp.arange(low, high, dtype=jnp.int32)
        target_hits = local_target[:, None] == vocab_iota[None, :]
        part_maxima = jnp.max(logits, axis=1)
        shifted = logits - part_maxima[:, None]
        weights = jnp.exp(shifted)
        parts.append(
            jnp.stack(
                [
                    part_maxima,
                    jnp.sum(weights, axis=1),
                    jnp.sum(weights * shifted, axis=1),
                    jnp.sum(jnp.where(target_hits, logits, 0.0), axis=1),
                ],
                axis=1,
            )
        )
    stats = jnp.stack(parts, axis=1)
    gathered = lax.all_to_all(stats.reshape(devices, owned_count, 2, 4), TENSOR, 0, 0, tiled=True)
    gathered = gathered.transpose(0, 2, 1, 3).reshape(devices * 2, owned_count, 4)
    part_max = gathered[:, :, 0]
    maxima = jnp.max(part_max, axis=0)
    gap = part_max - maxima[None, :]
    scale = jnp.exp(gap)
    totals = jnp.sum(scale * gathered[:, :, 1], axis=0)
    weighted = jnp.sum(scale * (gathered[:, :, 2] + gap * gathered[:, :, 1]), axis=0)
    target_logit = jnp.sum(gathered[:, :, 3], axis=0)
    own_index = lax.dynamic_slice_in_dim(scored_index, offset, owned_count)
    own_mask = lax.dynamic_slice_in_dim(slot_mask, offset, owned_count)
    segment = local_rows * devices // seq_lengths.shape[0]
    sequence = own_index // segment
    seq_iota = jnp.arange(seq_lengths.shape[0], dtype=jnp.int32)
    length_of = jnp.sum(
        jnp.where(sequence[:, None] == seq_iota[None, :], seq_lengths[None, :], 0), axis=1
    )
    live_slot = (own_mask == 1) & (own_index % segment < length_of)
    log_total = jnp.log(totals)
    logprob = jnp.where(live_slot, target_logit - maxima - log_total, 0.0)
    entropy = jnp.where(live_slot, log_total - weighted / totals, 0.0)
    return (logprob, entropy)


def split_mesh(mesh):
    grid = mesh.devices
    first = grid[0]
    coords = [getattr(d, "coords", None) for d in first]
    ring = len({c[1] for c in coords}) if all((c is not None for c in coords)) else 1
    return Mesh(grid.reshape(grid.shape[0], grid.shape[1] // ring, ring), ("dp", "tz", "ty"))


def solution(mesh):
    return jax.shard_map(
        body,
        mesh=split_mesh(mesh),
        in_specs=(
            P(("dp", "tz", "ty"), None),
            P(),
            P(),
            P(("tz", "ty"), "dp"),
            P("dp"),
            P("dp"),
            P("dp"),
            P("dp"),
        ),
        out_specs=(P(("dp", "tz", "ty")), P(("dp", "tz", "ty"))),
        check_vma=False,
    )
```

profile of v0, /device:TPU:2, one launch (start us, length us, event | category | flops | bytes accessed | tf_op | source)
XLA Modules:
  0.0 195.1 jit_solution(13988544709984714789)
XLA Ops:
  7.2 2.4 %slice.19 = bf16[1952,256]{1,0:T(8,128)(2,1)} slice(bf16[3920,256]{1,0:T(8,128)(2,1)} %param.11), slice={[0:1952], [0:256]} | slice | bytes 1998848 | tf_op jit(solution)/shard_map/slice | solution.py:64
  9.7 1.0 slice.20
  10.8 0.5 convolution_convert_fusion
  11.3 0.4 reshape.125
  11.7 0.5 copy.70
  12.2 19.4 %all_to_all.25 = bf16[4,16,4,2048]{3,2,1,0:T(4,128)(2,1)S(1)} all-to-all(bf16[4,16,4,2048]{3,2,1,0:T(4,128)(2,1)S(1)} %bitcast.15), channel_id=1, replica_groups=mesh['dp'=8,'tz'=16,'ty'=4] {'ty'}, dimensions={0} | all-to-all | bytes 2097152 | tf_op jit(solution)/shard_map/all_to_all | solution.py:38
  31.6 0.7 reduce_sum.124
  32.3 32.5 %all_to_all.26 = bf16[16,4,2048]{2,1,0:T(4,128)(2,1)S(1)} all-to-all(bf16[16,4,2048]{2,1,0:T(4,128)(2,1)S(1)} %reduce_sum.124), channel_id=1, replica_groups=mesh['dp'=8,'tz'=16,'ty'=4] {'tz'}, dimensions={0} | all-to-all | bytes 524288 | tf_op jit(solution)/shard_map/all_to_all | solution.py:40
  64.9 0.4 convert_reduce_fusion
  65.3 0.2 multiply_reduce_fusion
  65.7 22.5 %all_to_all.27 = bf16[16,4,2048]{2,1,0:T(4,128)(2,1)S(1)} all-to-all(bf16[16,4,2048]{2,1,0:T(4,128)(2,1)S(1)} %broadcast_in_dim.26), channel_id=1, replica_groups=mesh['dp'=8,'tz'=16,'ty'=4] {'tz'}, dimensions={0} | all-to-all | bytes 524288 | tf_op jit(solution)/shard_map/all_to_all | solution.py:43
  88.2 1.5 broadcast_in_dim.27
  89.7 3.5 %all-to-all-start.3 = ((bf16[4,16,4,2048]{3,2,1,0:T(4,128)(2,1)}), bf16[4,16,4,2048]{3,2,1,0:T(4,128)(2,1)S(1)}, u32[]{:S(2)}, u32[]{:S(2)}) async-start(bf16[4,16,4,2048]{3,2,1,0:T(4,128)(2,1)} %broadcast_in_dim.27), calls=%async_computation.3 | async-start | bytes 2097152 | tf_op jit(solution)/shard_map/all_to_all | solution.py:50
  93.2 10.8 %all-to-all-done.3 = bf16[4,16,4,2048]{3,2,1,0:T(4,128)(2,1)S(1)} async-done(((bf16[4,16,4,2048]{3,2,1,0:T(4,128)(2,1)}), bf16[4,16,4,2048]{3,2,1,0:T(4,128)(2,1)S(1)}, u32[]{:S(2)}, u32[]{:S(2)}) %all-to-all-start.3) | async-done | bytes 1048608 | tf_op jit(solution)/shard_map/all_to_all | solution.py:50
  104.0 0.6 copy.56
  104.6 1.1 reshape.126
  105.7 6.0 %fusion.4 = (f32[256]{0:T(256)S(1)}, f32[256,1952]{0,1:T(8,128)S(1)}) fusion(bf16[256,2048]{1,0:T(8,128)(2,1)} %reshape.126, bf16[1952,2048]{1,0:T(8,128)(2,1)} %all-gather.3.cloned.1.call-done), kind=kOutput, calls=%fused_computation.40 | convolution fusion | flops 2047319808 | bytes 11043840 | tf_op jit(solution)/shard_map/dot_general | solution.py:19
  111.9 0.7 exponential_reduce_fusion.1
  112.7 0.1 stack.37
  113.2 24.7 %all-gather.5.cloned.1.call-done = bf16[1968,2048]{1,0:T(8,128)(2,1)} async-done(((bf16[1968,256]{1,0:T(8,128)(2,1)}), bf16[1968,2048]{1,0:T(8,128)(2,1)}) %all-gather.5.cloned.1.call-update) | async-done | bytes 8060944 | tf_op jit(solution)/shard_map/all_gather | solution.py:64
  137.9 6.1 %fusion.3 = (f32[256]{0:T(256)S(1)}, f32[256,1968]{0,1:T(8,128)S(1)}) fusion(bf16[256,2048]{1,0:T(8,128)(2,1)} %reshape.126, bf16[1968,2048]{1,0:T(8,128)(2,1)} %all-gather.5.cloned.1.call-done), kind=kOutput, calls=%fused_computation.39 | convolution fusion | flops 2064101120 | bytes 11125760 | tf_op jit(solution)/shard_map/dot_general | solution.py:19
  144.1 1.0 exponential_reduce_fusion
  145.3 0.1 stack.42
  145.5 0.1 stack.41
  145.8 0.9 copy.65
  146.7 15.6 %all-to-all-start.4 = ((f32[64,4,2,4]{1,3,2,0:T(4,128)}), f32[64,4,2,4]{1,3,2,0:T(4,128)S(1)}, u32[]{:S(2)}, u32[]{:S(2)}) async-start(f32[64,4,2,4]{1,3,2,0:T(4,128)} %copy.65), calls=%async_computation.4 | async-start | bytes 524288 | tf_op jit(solution)/shard_map/all_to_all | solution.py:83
  163.0 22.3 %all-to-all-done.4 = f32[64,4,2,4]{1,3,2,0:T(4,128)S(1)} async-done(((f32[64,4,2,4]{1,3,2,0:T(4,128)}), f32[64,4,2,4]{1,3,2,0:T(4,128)S(1)}, u32[]{:S(2)}, u32[]{:S(2)}) %all-to-all-start.4) | async-done | bytes 8224 | tf_op jit(solution)/shard_map/all_to_all | solution.py:83
  185.3 1.0 copy.66
  186.3 0.6 slice_reduce_fusion
  186.9 0.2 multiply_reduce_fusion.1
  187.1 0.6 subtract_select_fusion
  187.7 0.5 subtract_select_fusion.1
  (40 shorter events, 1.5 us)
Async XLA Ops:
  7.2 3.7 %copy-start = (bf16[128,2048]{1,0:T(8,128)(2,1)S(1)}, bf16[128,2048]{1,0:T(8,128)(2,1)}, u32[]{:S(2)}) copy-start(bf16[128,2048]{1,0:T(8,128)(2,1)} %param.8) | copy-start | bytes 1572868
  7.2 2.5 %copy-start.1 = (bf16[3920,256]{1,0:T(8,128)(2,1)S(1)}, bf16[3920,256]{1,0:T(8,128)(2,1)}, u32[]{:S(2)}) copy-start(bf16[3920,256]{1,0:T(8,128)(2,1)} %param.11) | copy-start | bytes 6021124
  7.2 98.6 %all-gather.3.cloned.1.call-start = ((), (), s32[]{:S(2)}) async-start(), calls=%async_computation.5 | async-start | bytes 8994816 | tf_op jit(solution)/shard_map/all_gather | solution.py:64
  9.6 1.2 copy-start.4
  9.7 128.2 %all-gather.5.cloned.1.call-start = ((), (), s32[]{:S(2)}) async-start(), calls=%async_computation.6 | async-start | bytes 9068544 | tf_op jit(solution)/shard_map/all_gather | solution.py:64
  12.2 53.3 %copy-start.2 = (f32[2048]{0:T(1024)S(1)}, f32[2048]{0:T(1024)}, u32[]{:S(2)}) copy-start(f32[2048]{0:T(1024)} %param.10) | copy-start | bytes 24580
  12.2 53.3 %copy-start.3 = (f32[2048]{0:T(1024)S(1)}, f32[2048]{0:T(1024)}, u32[]{:S(2)}) copy-start(f32[2048]{0:T(1024)} %param.9) | copy-start | bytes 24580
  65.7 27.5 %copy-start.5 = (s32[256]{0:T(256)S(1)}, s32[256]{0:T(256)}, u32[]{:S(2)}) copy-start(s32[256]{0:T(256)} %param.14) | copy-start | bytes 3076
  89.7 14.4 %all-to-all-start.3 = ((bf16[4,16,4,2048]{3,2,1,0:T(4,128)(2,1)}), bf16[4,16,4,2048]{3,2,1,0:T(4,128)(2,1)S(1)}, u32[]{:S(2)}, u32[]{:S(2)}) async-start(bf16[4,16,4,2048]{3,2,1,0:T(4,128)(2,1)} %broadcast_in_dim.27), calls=%async_computation.3 | async-start | bytes 2097152 | tf_op jit(solution)/shard_map/all_to_all | solution.py:50
  144.1 43.1 %copy-start.6 = (s32[256]{0:T(256)S(1)}, s32[256]{0:T(256)}, u32[]{:S(2)}) copy-start(s32[256]{0:T(256)} %param.15) | copy-start | bytes 3076
  146.7 38.6 %all-to-all-start.4 = ((f32[64,4,2,4]{1,3,2,0:T(4,128)}), f32[64,4,2,4]{1,3,2,0:T(4,128)S(1)}, u32[]{:S(2)}, u32[]{:S(2)}) async-start(f32[64,4,2,4]{1,3,2,0:T(4,128)} %copy.65), calls=%async_computation.4 | async-start | bytes 524288 | tf_op jit(solution)/shard_map/all_to_all | solution.py:83
Sparse Core Ops, SparseCore 0:
  10.1 64.3 all-gather.2
  76.6 61.1 all-gather.4
where the time goes:
time: 196 us; the launch traced here: 195 us
  blocking collectives  74.4 us (38%)
  waiting for transfers between devices  57.8 us (29%)
  starting transfers between devices  19.2 us (10%)
  between operations  15 us (8%)
  matrix products  12.6 us (6%)
  local copies, waits for them, and re-layouts  11 us (6%)
  other arithmetic  5.14 us (3%)
    all_to_all x1, blocking collectives, body(): arrived = lax.all_to_all(near, 'tz', 0, 0, tiled=True)  32.5 us
    all_gather x2, waiting for transfers between devices, body(): lax.all_gather(head_table[low:high], 'dp', axis=1, tiled=True)  24.7 us
    all_to_all x1, blocking collectives, body(): lax.all_to_all(jnp.broadcast_to(owned_normed[None], (devices // ring, own...  22.5 us
    all_to_all x1, waiting for transfers between devices, body(): lax.all_to_all(stats.reshape(devices, owned_count, 2, 4), TENSOR, 0, 0, t...  22.3 us
    all_to_all x1, blocking collectives, body(): near = lax.all_to_all(by_y, 'ty', 0, 0, tiled=True)  19.4 us
    all_to_all x1, starting transfers between devices, body(): lax.all_to_all(stats.reshape(devices, owned_count, 2, 4), TENSOR, 0, 0, t...  15.6 us
    dot_general x2, matrix products, contract_last(): lax.dot_general(left, right, (((1,), (1,)), ((), ())), preferred_element_...  12.1 us
    all_to_all x1, waiting for transfers between devices, body(): lax.all_to_all(jnp.broadcast_to(along_z[None], (ring, devices // ring, ow...  10.8 us
  transfers between devices with their start and end apart: 4, of which 3 were waited for; matrix products, arithmetic and copies ran while one was open for 7% of the time, Pallas kernels for 0%

commit v1 on v0

--- a/solution.py
+++ b/solution.py
@@ -5,6 +5,27 @@
 
 EPSILON = 1e-05
 TENSOR = ("tz", "ty")
+
+
+def collect(shard, axis, dim):
+    size, index, span = (lax.axis_size(axis), lax.axis_index(axis), shard.shape[dim])
+    forward = [(i, (i + 1) % size) for i in range(size)]
+    left = [(i, (i - 1) % size) for i in range(size)]
+    out = jnp.zeros((*shard.shape[:dim], size * span, *shard.shape[dim + 1 :]), shard.dtype)
+    out = lax.dynamic_update_slice_in_dim(out, shard, index * span, axis=dim)
+    from_left = from_right = shard
+    middle = size // 2
+    for step in range(1, middle + 1):
+        from_left = lax.ppermute(from_left, axis, forward)
+        out = lax.dynamic_update_slice_in_dim(
+            out, from_left, (index - step) % size * span, axis=dim
+        )
+        if step < size - middle:
+            from_right = lax.ppermute(from_right, axis, left)
+            out = lax.dynamic_update_slice_in_dim(
+                out, from_right, (index + step) % size * span, axis=dim
+            )
+    return out
 
 
 def layer_norm(states, norm_gain, norm_bias):
@@ -60,9 +81,7 @@
     local_target = targets - position * vocab_local
     parts = []
     for low, high in ((0, split), (split, vocab_local)):
-        logits = contract_last(
-            chosen, lax.all_gather(head_table[low:high], "dp", axis=1, tiled=True)
-        )
+        logits = contract_last(chosen, collect(head_table[low:high], "dp", 1))
         vocab_iota = jnp.arange(low, high, dtype=jnp.int32)
         target_hits = local_target[:, None] == vocab_iota[None, :]
         part_maxima = jnp.max(logits, axis=1)

time: 196 us -> 171 us (0.87)
  the two profiles are of different devices: /device:TPU:2 before, /device:TPU:7 now
where the time goes in v1:
time: 171 us; the launch traced here: 170 us
  starting transfers between devices  66.5 us (39%)
  local copies, waits for them, and re-layouts  52.7 us (31%)
  waiting for transfers between devices  31.5 us (18%)
  matrix products  12.3 us (7%)
  other arithmetic  5.79 us (3%)
    ppermute x8, starting transfers between devices, collect(): from_left = lax.ppermute(from_left, axis, forward)  24.6 us
    all_to_all x1, waiting for transfers between devices, body(): lax.all_to_all(stats.reshape(devices, owned_count, 2, 4), TENSOR, 0, 0, t...  21.2 us
    dynamic_update_slice x8, local copies, waits for them, and re-layouts, collect(): lax.dynamic_update_slice_in_dim(out, from_left, (index - step) % size * s...  18.6 us
    dynamic_update_slice x6, local copies, waits for them, and re-layouts, collect(): lax.dynamic_update_slice_in_dim(out, from_right, (index + step) % size *...  12.7 us
    all_to_all x1, starting transfers between devices, body(): lax.all_to_all(stats.reshape(devices, owned_count, 2, 4), TENSOR, 0, 0, t...  12.5 us
    dot_general x2, matrix products, contract_last(): lax.dot_general(left, right, (((1,), (1,)), ((), ())), preferred_element_...  11.8 us
    all_to_all x1, starting transfers between devices, body(): lax.all_to_all(jnp.broadcast_to(owned_normed[None], (devices // ring, own...  11.7 us
    all_to_all x1, starting transfers between devices, body(): arrived = lax.all_to_all(near, 'tz', 0, 0, tiled=True)  10.4 us
  transfers between devices with their start and end apart: 19, of which 4 were waited for; matrix products, arithmetic and copies ran while one was open for 29% of the time, Pallas kernels for 0%

profile of v1, /device:TPU:7, one launch (start us, length us, event | category | flops | bytes accessed | tf_op | source)
XLA Modules:
  0.0 170.4 jit_solution(5661257417673574939)
XLA Ops:
  0.7 4.2 %broadcast_in_dim.32 = bf16[1952,2048]{1,0:T(8,128)(2,1)} broadcast(bf16[]{:T(256)} %constant.117.clone.1), dimensions={} | broadcast | bytes 7995394 | tf_op jit(solution)/shard_map/broadcast_in_dim | solution.py:14
  4.9 2.7 %fusion.3 = (bf16[1952,256]{1,0:T(8,128)(2,1)}, bf16[1952,2048]{1,0:T(8,128)(2,1)}) fusion(bf16[3920,256]{1,0:T(8,128)(2,1)} %param.11, bf16[1952,2048]{1,0:T(8,128)(2,1)} %broadcast_in_dim.32, s32[]{:T(128)S(6)} %select_n.116), kind=kLoop, calls=%fused_computation.55 | loop fusion | bytes 2998276 | tf_op jit(solution)/shard_map/slice | solution.py:84
  7.6 6.1 %collective-permute-start = (bf16[1952,256]{1,0:T(8,128)(2,1)}, bf16[1952,256]{1,0:T(8,128)(2,1)}, u32[]{:S(2)}, u32[]{:S(2)}) collective-permute-start(bf16[1952,256]{1,0:T(8,128)(2,1)} %get-tuple-element.19), channel_id=1, source_target_pairs={{0,64},{64,128},{128,192},{192,256},{256,320},{320,384},{384,448},... | collective-permute-start | bytes 2998280 | tf_op jit(solution)/shard_map/ppermute | solution.py:19
  16.2 3.5 %all-to-all-start = ((bf16[4,16,4,2048]{3,2,1,0:T(4,128)(2,1)}), bf16[4,16,4,2048]{3,2,1,0:T(4,128)(2,1)S(1)}, u32[]{:S(2)}, u32[]{:S(2)}) async-start(bf16[4,16,4,2048]{3,2,1,0:T(4,128)(2,1)} %bitcast.11), calls=%async_computation | async-start | bytes 2097152 | tf_op jit(solution)/shard_map/all_to_all | solution.py:59
  19.7 4.1 %broadcast_in_dim.64 = bf16[1968,2048]{1,0:T(8,128)(2,1)} broadcast(bf16[]{:T(256)} %constant.117.clone.1), dimensions={} | broadcast | bytes 8060930 | tf_op jit(solution)/shard_map/broadcast_in_dim | solution.py:14
  25.0 3.0 %collective-permute-start.7 = (bf16[1968,256]{1,0:T(8,128)(2,1)S(1)}, bf16[1968,256]{1,0:T(8,128)(2,1)}, u32[]{:S(2)}, u32[]{:S(2)}) collective-permute-start(bf16[1968,256]{1,0:T(8,128)(2,1)S(1)} %get-tuple-element.21), channel_id=1, source_target_pairs={{0,64},{64,128},{128,192},{192,256},{256,320},{320,384},{384,448},... | collective-permute-start | bytes 3022856 | tf_op jit(solution)/shard_map/ppermute | solution.py:19
  28.0 4.7 %all-to-all-done = bf16[4,16,4,2048]{3,2,1,0:T(4,128)(2,1)S(1)} async-done(((bf16[4,16,4,2048]{3,2,1,0:T(4,128)(2,1)}), bf16[4,16,4,2048]{3,2,1,0:T(4,128)(2,1)S(1)}, u32[]{:S(2)}, u32[]{:S(2)}) %all-to-all-start) | async-done | bytes 1048608 | tf_op jit(solution)/shard_map/all_to_all | solution.py:59
  34.1 10.4 %all-to-all-start.1 = ((bf16[16,4,2048]{2,1,0:T(4,128)(2,1)}), bf16[16,4,2048]{2,1,0:T(4,128)(2,1)S(1)}, u32[]{:S(2)}, u32[]{:S(2)}) async-start(bf16[16,4,2048]{2,1,0:T(4,128)(2,1)} %reduce_sum.124), calls=%async_computation.1 | async-start | bytes 524288 | tf_op jit(solution)/shard_map/all_to_all | solution.py:61
  44.5 4.3 %collective-permute-start.2 = (bf16[1952,256]{1,0:T(8,128)(2,1)}, bf16[1952,256]{1,0:T(8,128)(2,1)}, u32[]{:S(2)}, u32[]{:S(2)}) collective-permute-start(bf16[1952,256]{1,0:T(8,128)(2,1)} %collective-permute-done), channel_id=1, source_target_pairs={{0,64},{64,128},{128,192},{192,256},{256,320},{320,384},{384,448},... | collective-permute-start | bytes 2998280 | tf_op jit(solution)/shard_map/ppermute | solution.py:19
  48.8 2.3 %constant_dynamic-update-slice_fusion.14 = bf16[1952,2048]{1,0:T(8,128)(2,1)} fusion(bf16[1952,2048]{1,0:T(8,128)(2,1)} %get-tuple-element.20, bf16[1952,256]{1,0:T(8,128)(2,1)} %collective-permute-done, s32[]{:T(128)S(6)} %select_n.118), kind=kLoop, calls=%fused_computation.38 | loop fusion | bytes 1998852 | tf_op jit(solution)/shard_map/dynamic_update_slice | solution.py:20
  53.4 3.0 %collective-permute-start.9 = (bf16[1968,256]{1,0:T(8,128)(2,1)}, bf16[1968,256]{1,0:T(8,128)(2,1)}, u32[]{:S(2)}, u32[]{:S(2)}) collective-permute-start(bf16[1968,256]{1,0:T(8,128)(2,1)} %collective-permute-done.7), channel_id=1, source_target_pairs={{0,64},{64,128},{128,192},{192,256},{256,320},{320,384},{384,448},... | collective-permute-start | bytes 3022856 | tf_op jit(solution)/shard_map/ppermute | solution.py:19
  56.4 2.4 %constant_dynamic-update-slice_fusion.6 = bf16[1968,2048]{1,0:T(8,128)(2,1)} fusion(bf16[1968,2048]{1,0:T(8,128)(2,1)} %get-tuple-element.22, bf16[1968,256]{1,0:T(8,128)(2,1)} %collective-permute-done.7, s32[]{:T(128)S(6)} %select_n.118), kind=kLoop, calls=%fused_computation.30 | loop fusion | bytes 2015236 | tf_op jit(solution)/shard_map/dynamic_update_slice | solution.py:20
  58.7 2.3 %constant_dynamic-update-slice_fusion.5 = bf16[1968,2048]{1,0:T(8,128)(2,1)} fusion(bf16[1968,2048]{1,0:T(8,128)(2,1)} %constant_dynamic-update-slice_fusion.6, bf16[1968,256]{1,0:T(8,128)(2,1)} %collective-permute-done.8, s32[]{:T(128)S(6)} %select_n.120), kind=kLoop, calls=%fused_computation.29 | loop fusion | bytes 2015236 | tf_op jit(solution)/shard_map/dynamic_update_slice | solution.py:25
  62.6 11.7 %all-to-all-start.2 = ((bf16[16,4,2048]{2,1,0:T(4,128)(2,1)}), bf16[16,4,2048]{2,1,0:T(4,128)(2,1)S(1)}, u32[]{:S(2)}, u32[]{:S(2)}) async-start(bf16[16,4,2048]{2,1,0:T(4,128)(2,1)} %broadcast_in_dim.30), calls=%async_computation.2 | async-start | bytes 524288 | tf_op jit(solution)/shard_map/all_to_all | solution.py:64
  74.3 3.2 %collective-permute-start.4 = (bf16[1952,256]{1,0:T(8,128)(2,1)}, bf16[1952,256]{1,0:T(8,128)(2,1)}, u32[]{:S(2)}, u32[]{:S(2)}) collective-permute-start(bf16[1952,256]{1,0:T(8,128)(2,1)} %collective-permute-done.2), channel_id=1, source_target_pairs={{0,64},{64,128},{128,192},{192,256},{256,320},{320,384},{384,448},... | collective-permute-start | bytes 2998280 | tf_op jit(solution)/shard_map/ppermute | solution.py:19
  77.5 2.3 %constant_dynamic-update-slice_fusion.12 = bf16[1952,2048]{1,0:T(8,128)(2,1)} fusion(bf16[1952,2048]{1,0:T(8,128)(2,1)} %constant_dynamic-update-slice_fusion.13, bf16[1952,256]{1,0:T(8,128)(2,1)} %collective-permute-done.2, s32[]{:T(128)S(6)} %select_n.122), kind=kLoop, calls=%fused_computation.36 | loop fusion | bytes 1998852 | tf_op jit(solution)/shard_map/dynamic_update_slice | solution.py:20
  79.8 2.9 %collective-permute-start.11 = (bf16[1968,256]{1,0:T(8,128)(2,1)}, bf16[1968,256]{1,0:T(8,128)(2,1)}, u32[]{:S(2)}, u32[]{:S(2)}) collective-permute-start(bf16[1968,256]{1,0:T(8,128)(2,1)} %collective-permute-done.9), channel_id=1, source_target_pairs={{0,64},{64,128},{128,192},{192,256},{256,320},{320,384},{384,448},... | collective-permute-start | bytes 3022856 | tf_op jit(solution)/shard_map/ppermute | solution.py:19
  82.8 2.3 %constant_dynamic-update-slice_fusion.11 = bf16[1952,2048]{1,0:T(8,128)(2,1)} fusion(bf16[1952,2048]{1,0:T(8,128)(2,1)} %constant_dynamic-update-slice_fusion.12, bf16[1952,256]{1,0:T(8,128)(2,1)} %collective-permute-done.3, s32[]{:T(128)S(6)} %select_n.124), kind=kLoop, calls=%fused_computation.35 | loop fusion | bytes 1998852 | tf_op jit(solution)/shard_map/dynamic_update_slice | solution.py:25
  85.1 2.3 %constant_dynamic-update-slice_fusion.4 = bf16[1968,2048]{1,0:T(8,128)(2,1)} fusion(bf16[1968,2048]{1,0:T(8,128)(2,1)} %constant_dynamic-update-slice_fusion.5, bf16[1968,256]{1,0:T(8,128)(2,1)} %collective-permute-done.9, s32[]{:T(128)S(6)} %select_n.122), kind=kLoop, calls=%fused_computation.28 | loop fusion | bytes 2015236 | tf_op jit(solution)/shard_map/dynamic_update_slice | solution.py:20
  88.5 3.0 %all-to-all-done.2 = bf16[16,4,2048]{2,1,0:T(4,128)(2,1)S(1)} async-done(((bf16[16,4,2048]{2,1,0:T(4,128)(2,1)}), bf16[16,4,2048]{2,1,0:T(4,128)(2,1)S(1)}, u32[]{:S(2)}, u32[]{:S(2)}) %all-to-all-start.2) | async-done | bytes 262176 | tf_op jit(solution)/shard_map/all_to_all | solution.py:64
  93.0 3.7 %all-to-all-start.3 = ((bf16[4,16,4,2048]{3,2,1,0:T(4,128)(2,1)}), bf16[4,16,4,2048]{3,2,1,0:T(4,128)(2,1)S(1)}, u32[]{:S(2)}, u32[]{:S(2)}) async-start(bf16[4,16,4,2048]{3,2,1,0:T(4,128)(2,1)} %broadcast_in_dim.31), calls=%async_computation.3 | async-start | bytes 2097152 | tf_op jit(solution)/shard_map/all_to_all | solution.py:71
  98.7 2.4 %constant_dynamic-update-slice_fusion.10 = bf16[1952,2048]{1,0:T(8,128)(2,1)} fusion(bf16[1952,2048]{1,0:T(8,128)(2,1)} %constant_dynamic-update-slice_fusion.11, bf16[1952,256]{1,0:T(8,128)(2,1)} %collective-permute-done.4, s32[]{:T(128)S(6)} %select_n.126), kind=kLoop, calls=%fused_computation.34 | loop fusion | bytes 1998852 | tf_op jit(solution)/shard_map/dynamic_update_slice | solution.py:20
  101.1 2.3 %constant_dynamic-update-slice_fusion.9 = bf16[1952,2048]{1,0:T(8,128)(2,1)} fusion(bf16[1952,2048]{1,0:T(8,128)(2,1)} %constant_dynamic-update-slice_fusion.10, bf16[1952,256]{1,0:T(8,128)(2,1)} %collective-permute-done.5, s32[]{:T(128)S(6)} %select_n.128), kind=kLoop, calls=%fused_computation.33 | loop fusion | bytes 1998852 | tf_op jit(solution)/shard_map/dynamic_update_slice | solution.py:25
  103.5 2.3 %constant_dynamic-update-slice_fusion.2 = bf16[1968,2048]{1,0:T(8,128)(2,1)} fusion(bf16[1968,2048]{1,0:T(8,128)(2,1)} %constant_dynamic-update-slice_fusion.3, bf16[1968,256]{1,0:T(8,128)(2,1)} %collective-permute-done.11, s32[]{:T(128)S(6)} %select_n.126), kind=kLoop, calls=%fused_computation.26 | loop fusion | bytes 2015236 | tf_op jit(solution)/shard_map/dynamic_update_slice | solution.py:20
  105.9 2.3 %constant_dynamic-update-slice_fusion.1 = bf16[1968,2048]{1,0:T(8,128)(2,1)} fusion(bf16[1968,2048]{1,0:T(8,128)(2,1)} %constant_dynamic-update-slice_fusion.2, bf16[1968,256]{1,0:T(8,128)(2,1)} %collective-permute-done.12, s32[]{:T(128)S(6)} %select_n.128), kind=kLoop, calls=%fused_computation.25 | loop fusion | bytes 2015236 | tf_op jit(solution)/shard_map/dynamic_update_slice | solution.py:25
  108.1 2.6 %all-to-all-done.3 = bf16[4,16,4,2048]{3,2,1,0:T(4,128)(2,1)S(1)} async-done(((bf16[4,16,4,2048]{3,2,1,0:T(4,128)(2,1)}), bf16[4,16,4,2048]{3,2,1,0:T(4,128)(2,1)S(1)}, u32[]{:S(2)}, u32[]{:S(2)}) %all-to-all-start.3) | async-done | bytes 1048608 | tf_op jit(solution)/shard_map/all_to_all | solution.py:71
  112.4 2.3 %constant_dynamic-update-slice_fusion.8 = bf16[1952,2048]{1,0:T(8,128)(2,1)} fusion(bf16[1952,2048]{1,0:T(8,128)(2,1)} %constant_dynamic-update-slice_fusion.9, bf16[1952,256]{1,0:T(8,128)(2,1)} %collective-permute-done.6, s32[]{:T(128)S(6)} %select_n.130), kind=kLoop, calls=%fused_computation.32 | loop fusion | bytes 1998852 | tf_op jit(solution)/shard_map/dynamic_update_slice | solution.py:20
  114.7 5.9 %fusion.6 = (f32[256]{0:T(256)S(1)}, f32[256,1952]{0,1:T(8,128)S(1)}) fusion(bf16[256,2048]{1,0:T(8,128)(2,1)} %reshape.126, bf16[1952,2048]{1,0:T(8,128)(2,1)} %constant_dynamic-update-slice_fusion.8), kind=kOutput, calls=%fused_computation.58 | convolution fusion | flops 2047319808 | bytes 11043840 | tf_op jit(solution)/shard_map/dot_general | solution.py:40
  122.0 2.4 %constant_dynamic-update-slice_fusion = bf16[1968,2048]{1,0:T(8,128)(2,1)} fusion(bf16[1968,2048]{1,0:T(8,128)(2,1)} %constant_dynamic-update-slice_fusion.1, bf16[1968,256]{1,0:T(8,128)(2,1)} %collective-permute-done.13, s32[]{:T(128)S(6)} %select_n.130), kind=kLoop, calls=%fused_computation.24 | loop fusion | bytes 2015236 | tf_op jit(solution)/shard_map/dynamic_update_slice | solution.py:20
  124.4 6.0 %fusion.5 = (f32[256]{0:T(256)S(1)}, f32[256,1968]{0,1:T(8,128)S(1)}) fusion(bf16[256,2048]{1,0:T(8,128)(2,1)} %reshape.126, bf16[1968,2048]{1,0:T(8,128)(2,1)} %constant_dynamic-update-slice_fusion), kind=kOutput, calls=%fused_computation.57 | convolution fusion | flops 2064101120 | bytes 11125760 | tf_op jit(solution)/shard_map/dot_general | solution.py:40
  133.0 12.5 %all-to-all-start.4 = ((f32[64,4,2,4]{1,3,2,0:T(4,128)}), f32[64,4,2,4]{1,3,2,0:T(4,128)S(1)}, u32[]{:S(2)}, u32[]{:S(2)}) async-start(f32[64,4,2,4]{1,3,2,0:T(4,128)} %copy.65), calls=%async_computation.4 | async-start | bytes 524288 | tf_op jit(solution)/shard_map/all_to_all | solution.py:102
  146.2 21.2 %all-to-all-done.4 = f32[64,4,2,4]{1,3,2,0:T(4,128)S(1)} async-done(((f32[64,4,2,4]{1,3,2,0:T(4,128)}), f32[64,4,2,4]{1,3,2,0:T(4,128)S(1)}, u32[]{:S(2)}, u32[]{:S(2)}) %all-to-all-start.4) | async-done | bytes 8224 | tf_op jit(solution)/shard_map/all_to_all | solution.py:102
  (81 shorter events, 22.3 us)
Async XLA Ops:
  0.6 13.1 %copy-start = (bf16[128,2048]{1,0:T(8,128)(2,1)S(1)}, bf16[128,2048]{1,0:T(8,128)(2,1)}, u32[]{:S(2)}) copy-start(bf16[128,2048]{1,0:T(8,128)(2,1)} %param.8) | copy-start | bytes 1572868
  0.6 13.0 %copy-start.4 = (s32[256]{0:T(256)S(1)}, s32[256]{0:T(256)}, u32[]{:S(2)}) copy-start(s32[256]{0:T(256)} %param.13) | copy-start | bytes 3076
  7.6 36.9 %collective-permute-start = (bf16[1952,256]{1,0:T(8,128)(2,1)}, bf16[1952,256]{1,0:T(8,128)(2,1)}, u32[]{:S(2)}, u32[]{:S(2)}) collective-permute-start(bf16[1952,256]{1,0:T(8,128)(2,1)} %get-tuple-element.19), channel_id=1, source_target_pairs={{0,64},{64,128},{128,192},{192,256},{256,320},{320,384},{384,448},... | collective-permute-start | bytes 2998280 | tf_op jit(solution)/shard_map/ppermute | solution.py:19
  13.7 35.1 %collective-permute-start.1 = (bf16[1952,256]{1,0:T(8,128)(2,1)}, bf16[1952,256]{1,0:T(8,128)(2,1)}, u32[]{:S(2)}, u32[]{:S(2)}) collective-permute-start(bf16[1952,256]{1,0:T(8,128)(2,1)} %get-tuple-element.19), channel_id=1, source_target_pairs={{0,448},{64,0},{128,64},{192,128},{256,192},{320,256},{384,320},{4... | collective-permute-start | bytes 2998280 | tf_op jit(solution)/shard_map/ppermute | solution.py:24
  14.6 13.4 %copy-start.5 = (s32[256]{0:T(256)S(1)}, s32[256]{0:T(256)}, u32[]{:S(2)}) copy-start(s32[256]{0:T(256)} %param.14) | copy-start | bytes 3076
  16.2 16.6 %all-to-all-start = ((bf16[4,16,4,2048]{3,2,1,0:T(4,128)(2,1)}), bf16[4,16,4,2048]{3,2,1,0:T(4,128)(2,1)S(1)}, u32[]{:S(2)}, u32[]{:S(2)}) async-start(bf16[4,16,4,2048]{3,2,1,0:T(4,128)(2,1)} %bitcast.11), calls=%async_computation | async-start | bytes 2097152 | tf_op jit(solution)/shard_map/all_to_all | solution.py:59
  19.7 4.2 %copy-start.1 = (bf16[3920,256]{1,0:T(8,128)(2,1)S(1)}, bf16[3920,256]{1,0:T(8,128)(2,1)}, u32[]{:S(2)}) copy-start(bf16[3920,256]{1,0:T(8,128)(2,1)} %param.11) | copy-start | bytes 6021124
  23.8 37.8 %copy-start.2 = (f32[2048]{0:T(1024)S(1)}, f32[2048]{0:T(1024)}, u32[]{:S(2)}) copy-start(f32[2048]{0:T(1024)} %param.10) | copy-start | bytes 24580
  23.8 37.8 %copy-start.3 = (f32[2048]{0:T(1024)S(1)}, f32[2048]{0:T(1024)}, u32[]{:S(2)}) copy-start(f32[2048]{0:T(1024)} %param.9) | copy-start | bytes 24580
  25.0 28.4 %collective-permute-start.7 = (bf16[1968,256]{1,0:T(8,128)(2,1)S(1)}, bf16[1968,256]{1,0:T(8,128)(2,1)}, u32[]{:S(2)}, u32[]{:S(2)}) collective-permute-start(bf16[1968,256]{1,0:T(8,128)(2,1)S(1)} %get-tuple-element.21), channel_id=1, source_target_pairs={{0,64},{64,128},{128,192},{192,256},{256,320},{320,384},{384,448},... | collective-permute-start | bytes 3022856 | tf_op jit(solution)/shard_map/ppermute | solution.py:19
  27.9 28.4 %collective-permute-start.8 = (bf16[1968,256]{1,0:T(8,128)(2,1)S(1)}, bf16[1968,256]{1,0:T(8,128)(2,1)}, u32[]{:S(2)}, u32[]{:S(2)}) collective-permute-start(bf16[1968,256]{1,0:T(8,128)(2,1)S(1)} %get-tuple-element.21), channel_id=1, source_target_pairs={{0,448},{64,0},{128,64},{192,128},{256,192},{320,256},{384,320},{4... | collective-permute-start | bytes 3022856 | tf_op jit(solution)/shard_map/ppermute | solution.py:24
  34.1 26.9 %all-to-all-start.1 = ((bf16[16,4,2048]{2,1,0:T(4,128)(2,1)}), bf16[16,4,2048]{2,1,0:T(4,128)(2,1)S(1)}, u32[]{:S(2)}, u32[]{:S(2)}) async-start(bf16[16,4,2048]{2,1,0:T(4,128)(2,1)} %reduce_sum.124), calls=%async_computation.1 | async-start | bytes 524288 | tf_op jit(solution)/shard_map/all_to_all | solution.py:61
  44.5 29.8 %collective-permute-start.2 = (bf16[1952,256]{1,0:T(8,128)(2,1)}, bf16[1952,256]{1,0:T(8,128)(2,1)}, u32[]{:S(2)}, u32[]{:S(2)}) collective-permute-start(bf16[1952,256]{1,0:T(8,128)(2,1)} %collective-permute-done), channel_id=1, source_target_pairs={{0,64},{64,128},{128,192},{192,256},{256,320},{320,384},{384,448},... | collective-permute-start | bytes 2998280 | tf_op jit(solution)/shard_map/ppermute | solution.py:19
  48.8 28.8 %collective-permute-start.3 = (bf16[1952,256]{1,0:T(8,128)(2,1)}, bf16[1952,256]{1,0:T(8,128)(2,1)}, u32[]{:S(2)}, u32[]{:S(2)}) collective-permute-start(bf16[1952,256]{1,0:T(8,128)(2,1)} %collective-permute-done.1), channel_id=1, source_target_pairs={{0,448},{64,0},{128,64},{192,128},{256,192},{320,256},{384,320},{4... | collective-permute-start | bytes 2998280 | tf_op jit(solution)/shard_map/ppermute | solution.py:24
  53.4 26.5 %collective-permute-start.9 = (bf16[1968,256]{1,0:T(8,128)(2,1)}, bf16[1968,256]{1,0:T(8,128)(2,1)}, u32[]{:S(2)}, u32[]{:S(2)}) collective-permute-start(bf16[1968,256]{1,0:T(8,128)(2,1)} %collective-permute-done.7), channel_id=1, source_target_pairs={{0,64},{64,128},{128,192},{192,256},{256,320},{320,384},{384,448},... | collective-permute-start | bytes 3022856 | tf_op jit(solution)/shard_map/ppermute | solution.py:19
  56.4 28.7 %collective-permute-start.10 = (bf16[1968,256]{1,0:T(8,128)(2,1)}, bf16[1968,256]{1,0:T(8,128)(2,1)S(1)}, u32[]{:S(2)}, u32[]{:S(2)}) collective-permute-start(bf16[1968,256]{1,0:T(8,128)(2,1)} %collective-permute-done.8), channel_id=1, source_target_pairs={{0,448},{64,0},{128,64},{192,128},{256,192},{320,256},{384,320},{4... | collective-permute-start | bytes 3022856 | tf_op jit(solution)/shard_map/ppermute | solution.py:24
  62.6 29.0 %all-to-all-start.2 = ((bf16[16,4,2048]{2,1,0:T(4,128)(2,1)}), bf16[16,4,2048]{2,1,0:T(4,128)(2,1)S(1)}, u32[]{:S(2)}, u32[]{:S(2)}) async-start(bf16[16,4,2048]{2,1,0:T(4,128)(2,1)} %broadcast_in_dim.30), calls=%async_computation.2 | async-start | bytes 524288 | tf_op jit(solution)/shard_map/all_to_all | solution.py:64
  74.3 22.4 %collective-permute-start.4 = (bf16[1952,256]{1,0:T(8,128)(2,1)}, bf16[1952,256]{1,0:T(8,128)(2,1)}, u32[]{:S(2)}, u32[]{:S(2)}) collective-permute-start(bf16[1952,256]{1,0:T(8,128)(2,1)} %collective-permute-done.2), channel_id=1, source_target_pairs={{0,64},{64,128},{128,192},{192,256},{256,320},{320,384},{384,448},... | collective-permute-start | bytes 2998280 | tf_op jit(solution)/shard_map/ppermute | solution.py:19
  77.5 23.6 %collective-permute-start.5 = (bf16[1952,256]{1,0:T(8,128)(2,1)}, bf16[1952,256]{1,0:T(8,128)(2,1)}, u32[]{:S(2)}, u32[]{:S(2)}) collective-permute-start(bf16[1952,256]{1,0:T(8,128)(2,1)} %collective-permute-done.3), channel_id=1, source_target_pairs={{0,448},{64,0},{128,64},{192,128},{256,192},{320,256},{384,320},{4... | collective-permute-start | bytes 2998280 | tf_op jit(solution)/shard_map/ppermute | solution.py:24
  79.8 23.6 %collective-permute-start.11 = (bf16[1968,256]{1,0:T(8,128)(2,1)}, bf16[1968,256]{1,0:T(8,128)(2,1)}, u32[]{:S(2)}, u32[]{:S(2)}) collective-permute-start(bf16[1968,256]{1,0:T(8,128)(2,1)} %collective-permute-done.9), channel_id=1, source_target_pairs={{0,64},{64,128},{128,192},{192,256},{256,320},{320,384},{384,448},... | collective-permute-start | bytes 3022856 | tf_op jit(solution)/shard_map/ppermute | solution.py:19
  85.1 20.8 %collective-permute-start.12 = (bf16[1968,256]{1,0:T(8,128)(2,1)S(1)}, bf16[1968,256]{1,0:T(8,128)(2,1)}, u32[]{:S(2)}, u32[]{:S(2)}) collective-permute-start(bf16[1968,256]{1,0:T(8,128)(2,1)S(1)} %collective-permute-done.10), channel_id=1, source_target_pairs={{0,448},{64,0},{128,64},{192,128},{256,192},{320,256},{384,320},{4... | collective-permute-start | bytes 3022856 | tf_op jit(solution)/shard_map/ppermute | solution.py:24
  93.0 17.7 %all-to-all-start.3 = ((bf16[4,16,4,2048]{3,2,1,0:T(4,128)(2,1)}), bf16[4,16,4,2048]{3,2,1,0:T(4,128)(2,1)S(1)}, u32[]{:S(2)}, u32[]{:S(2)}) async-start(bf16[4,16,4,2048]{3,2,1,0:T(4,128)(2,1)} %broadcast_in_dim.31), calls=%async_computation.3 | async-start | bytes 2097152 | tf_op jit(solution)/shard_map/all_to_all | solution.py:71
  96.7 15.7 %collective-permute-start.6 = (bf16[1952,256]{1,0:T(8,128)(2,1)}, bf16[1952,256]{1,0:T(8,128)(2,1)}, u32[]{:S(2)}, u32[]{:S(2)}) collective-permute-start(bf16[1952,256]{1,0:T(8,128)(2,1)} %collective-permute-done.4), channel_id=1, source_target_pairs={{0,64},{64,128},{128,192},{192,256},{256,320},{320,384},{384,448},... | collective-permute-start | bytes 2998280 | tf_op jit(solution)/shard_map/ppermute | solution.py:19
  103.5 18.6 %collective-permute-start.13 = (bf16[1968,256]{1,0:T(8,128)(2,1)}, bf16[1968,256]{1,0:T(8,128)(2,1)}, u32[]{:S(2)}, u32[]{:S(2)}) collective-permute-start(bf16[1968,256]{1,0:T(8,128)(2,1)} %collective-permute-done.11), channel_id=1, source_target_pairs={{0,64},{64,128},{128,192},{192,256},{256,320},{320,384},{384,448},... | collective-permute-start | bytes 3022856 | tf_op jit(solution)/shard_map/ppermute | solution.py:19
  124.4 44.9 %copy-start.6 = (s32[256]{0:T(256)S(1)}, s32[256]{0:T(256)}, u32[]{:S(2)}) copy-start(s32[256]{0:T(256)} %param.15) | copy-start | bytes 3076
  133.0 34.4 %all-to-all-start.4 = ((f32[64,4,2,4]{1,3,2,0:T(4,128)}), f32[64,4,2,4]{1,3,2,0:T(4,128)S(1)}, u32[]{:S(2)}, u32[]{:S(2)}) async-start(f32[64,4,2,4]{1,3,2,0:T(4,128)} %copy.65), calls=%async_computation.4 | async-start | bytes 524288 | tf_op jit(solution)/shard_map/all_to_all | solution.py:102
